TPU v7x, 128 devices: a whole 4x4x4 slice. The times are simulated.
128 devices in a mesh: coil: 8 (over y, x_hi), pencil: 16 (over z, x_lo, core).
Axes of the slice: x: 4 (x_hi: 2, x_lo: 2; x = x_hi * 2 + x_lo), y: 4, z: 4, core: 2. Of those that a mesh axis runs over, the one named last changes fastest.
Arguments:
- object_image: bfloat16 [32, 256, 1024], P(None, 'pencil'), may hold values from -6 to 6
- coil_maps: bfloat16 [64, 32, 256, 1024], P('coil', None, 'pencil'), may hold values from -0.75 to 0.75
- sample_mask: int32 [32, 256, 4], replicated, may hold values 0 or 1
Outputs:
- adjoint_image: float32 [32, 256, 1024], P('coil', 'pencil')
Inputs may be any that keep to these rules, and one draw needn't show every extreme that they name: `sample_mask`: 1 where the 128 readout samples of a segment are acquired.
All inputs are finite; a program needn't handle non-finite values.
Results may differ from a plain program's by a relative error of at most 0.01.
Values may be sent and summed in bfloat16 or wider, within the bound.
No kernel may reach another device: no remote copies, remote signals or barrier semaphores. Data moves between devices by JAX's collectives and lax.ppermute only.
A program may use at most 192 MiB of HBM per device.

v0:
```python
import math
import jax
import jax.numpy as jnp
from jax import lax
from jax.sharding import PartitionSpec as P


def dft_tables(length, direction):
    indices = jnp.arange(length, dtype=jnp.int32)
    phases = indices[:, None] * indices[None, :] % length
    angles = phases.astype(jnp.float32) * (2.0 * math.pi / length)
    factor = 1.0 / math.sqrt(length)
    cosine = (jnp.cos(angles) * factor).astype(jnp.bfloat16)
    sine_part = (direction * jnp.sin(angles) * factor).astype(jnp.bfloat16)
    return (cosine, sine_part)


def readout_table(length, direction):
    cosine, sine_part = dft_tables(length, direction)
    upper = jnp.concatenate([cosine, sine_part], axis=1)
    lower = jnp.concatenate([-sine_part, cosine], axis=1)
    return jnp.concatenate([upper, lower], axis=0)


def complex_product(left_side, right_side, readout, conjugate):
    left_full = left_side.astype(jnp.float32)
    right_full = right_side.astype(jnp.float32)
    left_real = left_full[..., :readout]
    left_imag = left_full[..., readout:]
    if conjugate:
        left_imag = -left_imag
    right_real = right_full[..., :readout]
    right_imag = right_full[..., readout:]
    real_part = left_real * right_real - left_imag * right_imag
    imag_part = left_real * right_imag + left_imag * right_real
    return jnp.concatenate([real_part, imag_part], axis=-1)


def transform(volume, tables, formula, readout):
    cosine, sine_part = tables
    direct = jnp.einsum(formula, cosine, volume, preferred_element_type=jnp.float32)
    crossed = jnp.einsum(formula, sine_part, volume, preferred_element_type=jnp.float32)
    turned = jnp.concatenate([-crossed[..., readout:], crossed[..., :readout]], axis=-1)
    return (direct + turned).astype(jnp.bfloat16)


def widen(mask_part, segment):
    flags = jnp.repeat(mask_part, segment, axis=2) > 0
    return jnp.concatenate([flags, flags], axis=2)


def on_device(object_image, coil_maps, sample_mask):
    readout = object_image.shape[2] // 2
    slices = object_image.shape[0]
    row_count = object_image.shape[1]
    pencils = lax.axis_size("pencil")
    depth = slices // pencils
    lines = row_count * pencils
    segment = readout // sample_mask.shape[2]
    position = lax.axis_index("pencil")
    forward_x = readout_table(readout, -1.0)
    inverse_x = readout_table(readout, 1.0)
    forward_z = dft_tables(slices, -1.0)
    inverse_z = dft_tables(slices, 1.0)
    forward_y = dft_tables(lines, -1.0)
    inverse_y = dft_tables(lines, 1.0)
    column_mask = widen(lax.dynamic_slice_in_dim(sample_mask, position * depth, depth, 0), segment)
    nothing = jnp.zeros((), jnp.bfloat16)
    coil_image = complex_product(coil_maps, object_image[None], readout, False).astype(jnp.bfloat16)
    volume = jnp.dot(coil_image, forward_x, preferred_element_type=jnp.float32).astype(jnp.bfloat16)
    volume = transform(volume, forward_z, "kz,czyx->ckyx", readout)
    spectrum = transform(
        lax.all_to_all(volume, "pencil", split_axis=1, concat_axis=2, tiled=True),
        forward_y,
        "ky,czyx->czkx",
        readout,
    )
    spectrum = jnp.where(column_mask, spectrum, nothing)
    spectrum = transform(spectrum, inverse_y, "ky,czyx->czkx", readout)
    coil_block = lax.all_to_all(spectrum, "pencil", split_axis=2, concat_axis=1, tiled=True)
    coil_block = transform(coil_block, inverse_z, "kz,czyx->ckyx", readout)
    returned = jnp.dot(coil_block, inverse_x, preferred_element_type=jnp.float32).astype(
        jnp.bfloat16
    )
    partial_sum = jnp.sum(complex_product(coil_maps, returned, readout, True), axis=0)
    summed = lax.psum(partial_sum.astype(jnp.bfloat16), "coil").astype(jnp.float32)
    share_rows = slices // lax.axis_size("coil")
    return lax.dynamic_slice_in_dim(summed, lax.axis_index("coil") * share_rows, share_rows, 0)


def solution(mesh):
    placed = (P(None, "pencil", None), P("coil", None, "pencil", None), P())
    return jax.shard_map(
        on_device, mesh=mesh, in_specs=placed, out_specs=P("coil", "pencil", None), check_vma=False
    )
```

profile of v0, /device:TPU:0, one launch (start us, length us, event | category | flops | bytes accessed | tf_op | source)
XLA Modules:
  0.0 600.3 jit_solution(16223874633150782746)
XLA Ops:
  14.9 11.5 %convert_element_type.120 = f32[8,32,16,1024]{3,2,1,0:T(8,128)} convert(bf16[8,32,16,1024]{3,2,1,0:T(8,128)(2,1)} %param.4) | non-fusion elementwise | flops 4194304 | bytes 25165824 | tf_op jit(solution)/shard_map/convert_element_type | solution.py:26
  26.9 7.5 %subtract_convert_fusion = (bf16[8,32,16,512]{3,2,1,0:T(8,128)(2,1)S(1)}, bf16[8,32,16,512]{3,2,1,0:T(8,128)(2,1)S(1)}) fusion(f32[8,32,16,1024]{3,2,1,0:T(8,128)} %convert_element_type.120, f32[32,16,512]{2,1,0:T(8,128)S(1)} %get-tuple-element.18, f32[32,16,512]{2,1,0:T(8,128)S(1)} %get-tuple-element.17), kind=kLoop, calls=%fused_computation.27 | loop fusion | flops 16777216 | bytes 27262976 | tf_op jit(solution)/shard_map/convert.1
  34.4 11.5 %fusion.14 = bf16[8,32,16,1024]{3,2,1,0:T(8,128)(2,1)} fusion(bf16[8,32,16,512]{3,2,1,0:T(8,128)(2,1)S(1)} %get-tuple-element.8, bf16[8,32,16,512]{3,2,1,0:T(8,128)(2,1)S(1)} %get-tuple-element.7, bf16[512,512]{1,0:T(8,128)(2,1)S(1)} %get-tuple-element.20, bf16[512,512]{1,0:T(8,128)(2,1)S(1)} %fusion.42, bf16[512,512]{1,0:T(8,128)(2,1)S(1)} %get-tuple-element.19), kind=kOutput, calls=%fused_computation.31 | convolution fusion | flops 8619294720 | bytes 18350080 | tf_op jit(solution)/shard_map/dot_general | solution.py:70
  45.9 15.0 %convolution_bitcast_fusion.1 = f32[8,32,16,1024]{3,1,2,0:T(8,128)S(1)} fusion(bf16[8,32,16,1024]{3,2,1,0:T(8,128)(2,1)} %fusion.14), kind=kOutput, calls=%fused_computation.10 | convolution fusion | flops 268451840 | bytes 25165824 | tf_op jit(solution)/shard_map/kz,czyx->ckyx/dot_general | solution.py:42
  61.0 6.8 %slice_negate_fusion.3 = (f32[8,32,16,512]{3,1,2,0:T(8,128)}, f32[8,32,16,512]{3,1,2,0:T(8,128)}) fusion(f32[8,32,16,1024]{3,1,2,0:T(8,128)S(1)} %convolution_bitcast_fusion.1), kind=kLoop, calls=%fused_computation.16 | loop fusion | flops 2097152 | bytes 33554432 | tf_op jit(solution)/shard_map/neg | solution.py:43
  67.8 26.7 %fusion = bf16[8,32,16,1024]{3,1,2,0:T(8,128)(2,1)} fusion(f32[8,32,16,512]{3,1,2,0:T(8,128)} %get-tuple-element.16, f32[8,32,16,512]{3,1,2,0:T(8,128)} %get-tuple-element.15, bf16[8,32,16,1024]{3,2,1,0:T(8,128)(2,1)} %fusion.14), kind=kOutput, calls=%fused_computation.1 | convolution fusion | flops 281034752 | bytes 33554432 | tf_op jit(solution)/shard_map/kz,czyx->ckyx/dot_general | solution.py:41
  94.5 11.3 %copy.28 = bf16[8,32,16,1024]{3,2,0,1:T(8,128)(2,1)} copy(bf16[8,32,16,1024]{3,1,2,0:T(8,128)(2,1)} %fusion) | data formatting | bytes 16777216 | tf_op jit(solution)/shard_map/convert_element_type | solution.py:44
  105.8 6.9 %all-to-all-start = ((bf16[8,32,16,1024]{3,2,0,1:T(8,128)(2,1)}), bf16[8,32,16,1024]{3,2,0,1:T(8,128)(2,1)}, u32[]{:S(2)}, u32[]{:S(2)}) async-start(bf16[8,32,16,1024]{3,2,0,1:T(8,128)(2,1)} %copy.28), calls=%async_computation | async-start | bytes 16777216 | tf_op jit(solution)/shard_map/all_to_all | solution.py:73
  113.6 94.4 %all-to-all-done = bf16[8,32,16,1024]{3,2,0,1:T(8,128)(2,1)} async-done(((bf16[8,32,16,1024]{3,2,0,1:T(8,128)(2,1)}), bf16[8,32,16,1024]{3,2,0,1:T(8,128)(2,1)}, u32[]{:S(2)}, u32[]{:S(2)}) %all-to-all-start) | async-done | bytes 8388640 | tf_op jit(solution)/shard_map/all_to_all | solution.py:73
  208.0 8.5 %copy.30 = bf16[8,2,16,16,1024]{4,3,2,1,0:T(8,128)(2,1)} copy(bf16[8,2,16,16,1024]{4,3,0,1,2:T(8,128)(2,1)} %bitcast.15) | data formatting | bytes 16777216 | tf_op jit(solution)/shard_map/all_to_all | solution.py:73
  229.6 13.8 %fusion.1 = bf16[8,2,256,1024]{2,3,1,0:T(8,128)(2,1)} fusion(f32[8,2,256,512]{2,3,1,0:T(8,128)} %get-tuple-element.14, f32[8,2,256,512]{2,3,1,0:T(8,128)} %get-tuple-element.13, bf16[8,2,256,1024]{3,2,1,0:T(8,128)(2,1)} %bitcast.80), kind=kOutput, calls=%fused_computation.3 | convolution fusion | flops 2161115136 | bytes 33554432 | tf_op jit(solution)/shard_map/ky,czyx->czkx/dot_general | solution.py:41
  250.0 6.9 %slice_negate_fusion.1 = (f32[8,2,256,512]{2,3,1,0:T(8,128)}, f32[8,2,256,512]{2,3,1,0:T(8,128)}) fusion(f32[8,2,256,1024]{2,3,1,0:T(8,128)S(1)} %convolution_bitcast_fusion.2), kind=kLoop, calls=%fused_computation.14 | loop fusion | flops 2097152 | bytes 33554432 | tf_op jit(solution)/shard_map/neg | solution.py:43
  256.9 13.7 %fusion.2 = bf16[8,2,256,1024]{2,3,1,0:T(8,128)(2,1)} fusion(f32[8,2,256,512]{2,3,1,0:T(8,128)} %get-tuple-element.12, f32[8,2,256,512]{2,3,1,0:T(8,128)} %get-tuple-element.11, bf16[8,2,256,1024]{2,3,1,0:T(8,128)(2,1)} %fusion.1, pred[2,256,1024]{1,2,0:T(8,128)(4,1)S(1)} %pad_add_fusion), kind=kOutput, calls=%fused_computation.5 | convolution fusion | flops 2165309440 | bytes 34078720 | tf_op jit(solution)/shard_map/ky,czyx->czkx/dot_general | solution.py:41
  270.6 21.2 %copy.33 = bf16[8,2,256,1024]{3,1,0,2:T(2,128)(2,1)} copy(bf16[8,2,256,1024]{2,3,1,0:T(8,128)(2,1)} %fusion.2) | data formatting | bytes 16777216 | tf_op jit(solution)/shard_map/convert_element_type | solution.py:44
  304.6 87.2 %all-to-all-done.1 = bf16[8,2,256,1024]{3,1,0,2:T(2,128)(2,1)} async-done(((bf16[8,2,256,1024]{3,1,0,2:T(2,128)(2,1)}), bf16[8,2,256,1024]{3,1,0,2:T(2,128)(2,1)}, u32[]{:S(2)}, u32[]{:S(2)}) %all-to-all-start.1) | async-done | bytes 8388640 | tf_op jit(solution)/shard_map/all_to_all | solution.py:80
  391.8 11.3 %copy.34 = bf16[8,2,256,1024]{3,2,1,0:T(8,128)(2,1)} copy(bf16[8,2,256,1024]{3,1,0,2:T(2,128)(2,1)} %all-to-all-done.1) | data formatting | bytes 16777216 | tf_op jit(solution)/shard_map/all_to_all | solution.py:80
  403.1 16.3 %copy.35 = bf16[8,16,2,16,1024]{4,2,1,3,0:T(2,128)(2,1)} copy(bf16[8,16,2,16,1024]{4,3,1,2,0:T(8,128)(2,1)} %bitcast.81) | data formatting | bytes 16777216 | tf_op jit(solution)/shard_map/all_to_all | solution.py:80
  419.5 13.2 %all_to_all.33 = bf16[8,32,16,1024]{3,1,2,0:T(8,128)(2,1)} reshape(bf16[8,16,2,16,1024]{4,2,1,3,0:T(2,128)(2,1)} %copy.35) | data formatting | bytes 16777216 | tf_op jit(solution)/shard_map/all_to_all | solution.py:80
  438.4 6.8 %slice_negate_fusion = (f32[8,32,16,512]{3,1,2,0:T(8,128)}, f32[8,32,16,512]{3,1,2,0:T(8,128)}) fusion(f32[8,32,16,1024]{3,1,2,0:T(8,128)S(1)} %convolution_bitcast_fusion), kind=kLoop, calls=%fused_computation.13 | loop fusion | flops 2097152 | bytes 33554432 | tf_op jit(solution)/shard_map/neg | solution.py:43
  445.2 12.0 %fusion.3 = bf16[8,32,16,1024]{3,1,2,0:T(8,128)(2,1)} fusion(f32[8,32,16,512]{3,1,2,0:T(8,128)} %get-tuple-element.10, f32[8,32,16,512]{3,1,2,0:T(8,128)} %get-tuple-element.9, bf16[8,32,16,1024]{3,1,2,0:T(8,128)(2,1)} %all_to_all.33), kind=kOutput, calls=%fused_computation.7 | convolution fusion | flops 281034752 | bytes 33554432 | tf_op jit(solution)/shard_map/kz,czyx->ckyx/dot_general | solution.py:41
  457.3 17.3 %convert_convert_fusion = f32[8,32,16,1024]{3,2,1,0:T(8,128)} fusion(bf16[8,32,16,1024]{3,1,2,0:T(8,128)(2,1)} %fusion.3, bf16[512,512]{1,0:T(8,128)(2,1)S(1)} %get-tuple-element.20, bf16[512,512]{1,0:T(8,128)(2,1)S(1)} %fusion.43, bf16[512,512]{1,0:T(8,128)(2,1)S(1)} %multiply_convert_fusion), kind=kOutput, calls=%fused_computation.25 | convolution fusion | flops 8606711808 | bytes 26738688 | tf_op jit(solution)/shard_map/dot_general | solution.py:82
  474.6 18.5 %multiply_subtract_fusion = (f32[8,32,16,512]{3,2,1,0:T(8,128)}, f32[8,32,16,512]{3,2,1,0:T(8,128)}) fusion(f32[8,32,16,1024]{3,2,1,0:T(8,128)} %convert_convert_fusion, f32[8,32,16,1024]{3,2,1,0:T(8,128)} %convert_element_type.120), kind=kLoop, calls=%fused_computation.24 | loop fusion | flops 14680064 | bytes 50331648 | tf_op jit(solution)/shard_map/sub | solution.py:34
  493.0 7.9 %maximum_reduce_fusion = bf16[32,16,1024]{2,1,0:T(8,128)(2,1)} fusion(f32[8,32,16,512]{3,2,1,0:T(8,128)} %get-tuple-element.6, f32[8,32,16,512]{3,2,1,0:T(8,128)} %get-tuple-element.5), kind=kLoop, calls=%fused_computation.8 | loop fusion | flops 7864320 | bytes 17825792 | tf_op jit(solution)/shard_map/reduce_sum | solution.py:85
  501.0 90.6 %all-reduce.2.cloned.1.call-done = bf16[32,16,1024]{2,1,0:T(8,128)(2,1)} async-done(((bf16[32,16,1024]{2,1,0:T(8,128)(2,1)}), bf16[32,16,1024]{2,1,0:T(8,128)(2,1)}) %all-reduce.2.cloned.1.call-update) | async-done | bytes 1048592 | tf_op jit(solution)/shard_map/psum | solution.py:86
  (19 shorter events, 49.7 us)
Async XLA Ops:
  14.9 11.5 %copy-start = (bf16[32,16,1024]{2,1,0:T(8,128)(2,1)S(1)}, bf16[32,16,1024]{2,1,0:T(8,128)(2,1)}, u32[]{:S(2)}) copy-start(bf16[32,16,1024]{2,1,0:T(8,128)(2,1)} %param.3) | copy-start | bytes 3145732
  105.8 102.2 %all-to-all-start = ((bf16[8,32,16,1024]{3,2,0,1:T(8,128)(2,1)}), bf16[8,32,16,1024]{3,2,0,1:T(8,128)(2,1)}, u32[]{:S(2)}, u32[]{:S(2)}) async-start(bf16[8,32,16,1024]{3,2,0,1:T(8,128)(2,1)} %copy.28), calls=%async_computation | async-start | bytes 16777216 | tf_op jit(solution)/shard_map/all_to_all | solution.py:73
  291.8 100.1 %all-to-all-start.1 = ((bf16[8,2,256,1024]{3,1,0,2:T(2,128)(2,1)}), bf16[8,2,256,1024]{3,1,0,2:T(2,128)(2,1)}, u32[]{:S(2)}, u32[]{:S(2)}) async-start(bf16[8,2,256,1024]{3,1,0,2:T(2,128)(2,1)} %copy.33), calls=%async_computation.1 | async-start | bytes 16777216 | tf_op jit(solution)/shard_map/all_to_all | solution.py:80
  296.5 295.1 %all-reduce.2.cloned.1.call-start = ((), (), s32[]{:S(2)}) async-start(), calls=%async_computation.2 | async-start | bytes 2097152 | tf_op jit(solution)/shard_map/psum | solution.py:86
Sparse Core Ops, SparseCore 0:
  501.1 90.4 all-reduce.1
where the time goes:
time: 608 us; the launch traced here: 600 us
  waiting for transfers between devices  272 us (45%)
  matrix products  129 us (21%)
  other arithmetic  91.2 us (15%)
  local copies, waits for them, and re-layouts  82.2 us (14%)
  between operations  13.8 us (2%)
  starting transfers between devices  11.7 us (2%)
    all_to_all x1, waiting for transfers between devices, on_device(): lax.all_to_all(volume, 'pencil', split_axis=1, concat_axis=2, tiled=True)  94.4 us
    psum x1, waiting for transfers between devices, on_device(): lax.psum(partial_sum.astype(jnp.bfloat16), 'coil').astype(jnp.float32)  90.6 us
    all_to_all x1, waiting for transfers between devices, on_device(): lax.all_to_all(spectrum, 'pencil', split_axis=2, concat_axis=1, tiled=True)  87.2 us
    dot_general x4, matrix products, transform(): jnp.einsum(formula, cosine, volume, preferred_element_type=jnp.float32)  66.2 us
    all_to_all x3, local copies, waits for them, and re-layouts, on_device(): lax.all_to_all(spectrum, 'pencil', split_axis=2, concat_axis=1, tiled=True)  40.8 us
    dot_general x4, matrix products, transform(): jnp.einsum(formula, sine_part, volume, preferred_element_type=jnp.float32)  34.2 us
    convert_element_type x2, local copies, waits for them, and re-layouts, transform(): return (direct + turned).astype(jnp.bfloat16)  32.5 us
    neg x4, other arithmetic, transform(): -crossed[..., readout:]  26.8 us
  transfers between devices with their start and end apart: 3, of which 3 were waited for; matrix products, arithmetic and copies ran while one was open for 1% of the time, Pallas kernels for 0%

commit v1 on v0

--- a/solution.py
+++ b/solution.py
@@ -83,7 +83,9 @@
         jnp.bfloat16
     )
     partial_sum = jnp.sum(complex_product(coil_maps, returned, readout, True), axis=0)
-    summed = lax.psum(partial_sum.astype(jnp.bfloat16), "coil").astype(jnp.float32)
+    summed = jnp.sum(lax.all_gather(partial_sum.astype(jnp.bfloat16), "coil"), axis=0).astype(
+        jnp.float32
+    )
     share_rows = slices // lax.axis_size("coil")
     return lax.dynamic_slice_in_dim(summed, lax.axis_index("coil") * share_rows, share_rows, 0)
 

time: 608 us -> 630 us (1.036)
  waiting for transfers between devices: 272 us -> 288 us
    all_gather x0 -> x1, waiting for transfers between devices: none -> 107 us  [on_device(): lax.all_gather(partial_sum.astype(jnp.bfloat16), 'coil')]
    psum x1 -> x0, waiting for transfers between devices: 90.6 us -> none  [on_device(): lax.psum(partial_sum.astype(jnp.bfloat16), 'coil').astype(jnp.float32)]
where the time goes in v1:
time: 630 us; the launch traced here: 622 us
  waiting for transfers between devices  288 us (46%)
  matrix products  129 us (20%)
  other arithmetic  96.3 us (15%)
  local copies, waits for them, and re-layouts  82.2 us (13%)
  between operations  14 us (2%)
  starting transfers between devices  11.7 us (2%)
    all_gather x1, waiting for transfers between devices, on_device(): lax.all_gather(partial_sum.astype(jnp.bfloat16), 'coil')  107 us
    all_to_all x1, waiting for transfers between devices, on_device(): lax.all_to_all(volume, 'pencil', split_axis=1, concat_axis=2, tiled=True)  94.4 us
    all_to_all x1, waiting for transfers between devices, on_device(): lax.all_to_all(spectrum, 'pencil', split_axis=2, concat_axis=1, tiled=True)  87.2 us
    dot_general x4, matrix products, transform(): jnp.einsum(formula, cosine, volume, preferred_element_type=jnp.float32)  66.2 us
    all_to_all x3, local copies, waits for them, and re-layouts, on_device(): lax.all_to_all(spectrum, 'pencil', split_axis=2, concat_axis=1, tiled=True)  40.8 us
    dot_general x4, matrix products, transform(): jnp.einsum(formula, sine_part, volume, preferred_element_type=jnp.float32)  34.2 us
    convert_element_type x2, local copies, waits for them, and re-layouts, transform(): return (direct + turned).astype(jnp.bfloat16)  32.5 us
    neg x4, other arithmetic, transform(): -crossed[..., readout:]  26.8 us
  transfers between devices with their start and end apart: 3, of which 3 were waited for; matrix products, arithmetic and copies ran while one was open for 1% of the time, Pallas kernels for 0%

profile of v1, /device:TPU:0, one launch (start us, length us, event | category | flops | bytes accessed | tf_op | source)
XLA Modules:
  0.0 621.8 jit_solution(3658111433401568009)
XLA Ops:
  14.9 11.5 %convert_element_type.132 = f32[8,32,16,1024]{3,2,1,0:T(8,128)} convert(bf16[8,32,16,1024]{3,2,1,0:T(8,128)(2,1)} %param.4) | non-fusion elementwise | flops 4194304 | bytes 25165824 | tf_op jit(solution)/shard_map/convert_element_type | solution.py:26
  26.9 7.5 %subtract_convert_fusion = (bf16[8,32,16,512]{3,2,1,0:T(8,128)(2,1)S(1)}, bf16[8,32,16,512]{3,2,1,0:T(8,128)(2,1)S(1)}) fusion(f32[8,32,16,1024]{3,2,1,0:T(8,128)} %convert_element_type.132, f32[32,16,512]{2,1,0:T(8,128)S(1)} %get-tuple-element.18, f32[32,16,512]{2,1,0:T(8,128)S(1)} %get-tuple-element.17), kind=kLoop, calls=%fused_computation.27 | loop fusion | flops 16777216 | bytes 27262976 | tf_op jit(solution)/shard_map/convert.2
  34.4 11.6 %fusion.14 = bf16[8,32,16,1024]{3,2,1,0:T(8,128)(2,1)} fusion(bf16[8,32,16,512]{3,2,1,0:T(8,128)(2,1)S(1)} %get-tuple-element.8, bf16[8,32,16,512]{3,2,1,0:T(8,128)(2,1)S(1)} %get-tuple-element.7, bf16[512,512]{1,0:T(8,128)(2,1)S(1)} %get-tuple-element.20, bf16[512,512]{1,0:T(8,128)(2,1)S(1)} %fusion.42, bf16[512,512]{1,0:T(8,128)(2,1)S(1)} %get-tuple-element.19), kind=kOutput, calls=%fused_computation.31 | convolution fusion | flops 8619294720 | bytes 18350080 | tf_op jit(solution)/shard_map/dot_general | solution.py:70
  46.0 15.0 %convolution_bitcast_fusion.1 = f32[8,32,16,1024]{3,1,2,0:T(8,128)S(1)} fusion(bf16[8,32,16,1024]{3,2,1,0:T(8,128)(2,1)} %fusion.14), kind=kOutput, calls=%fused_computation.10 | convolution fusion | flops 268451840 | bytes 25165824 | tf_op jit(solution)/shard_map/kz,czyx->ckyx/dot_general | solution.py:42
  61.1 6.8 %slice_negate_fusion.3 = (f32[8,32,16,512]{3,1,2,0:T(8,128)}, f32[8,32,16,512]{3,1,2,0:T(8,128)}) fusion(f32[8,32,16,1024]{3,1,2,0:T(8,128)S(1)} %convolution_bitcast_fusion.1), kind=kLoop, calls=%fused_computation.16 | loop fusion | flops 2097152 | bytes 33554432 | tf_op jit(solution)/shard_map/neg | solution.py:43
  67.8 26.7 %fusion = bf16[8,32,16,1024]{3,1,2,0:T(8,128)(2,1)} fusion(f32[8,32,16,512]{3,1,2,0:T(8,128)} %get-tuple-element.16, f32[8,32,16,512]{3,1,2,0:T(8,128)} %get-tuple-element.15, bf16[8,32,16,1024]{3,2,1,0:T(8,128)(2,1)} %fusion.14), kind=kOutput, calls=%fused_computation.1 | convolution fusion | flops 281034752 | bytes 33554432 | tf_op jit(solution)/shard_map/kz,czyx->ckyx/dot_general | solution.py:41
  94.5 11.3 %copy.28 = bf16[8,32,16,1024]{3,2,0,1:T(8,128)(2,1)} copy(bf16[8,32,16,1024]{3,1,2,0:T(8,128)(2,1)} %fusion) | data formatting | bytes 16777216 | tf_op jit(solution)/shard_map/convert_element_type | solution.py:44
  105.8 6.9 %all-to-all-start = ((bf16[8,32,16,1024]{3,2,0,1:T(8,128)(2,1)}), bf16[8,32,16,1024]{3,2,0,1:T(8,128)(2,1)}, u32[]{:S(2)}, u32[]{:S(2)}) async-start(bf16[8,32,16,1024]{3,2,0,1:T(8,128)(2,1)} %copy.28), calls=%async_computation | async-start | bytes 16777216 | tf_op jit(solution)/shard_map/all_to_all | solution.py:73
  113.7 94.4 %all-to-all-done = bf16[8,32,16,1024]{3,2,0,1:T(8,128)(2,1)} async-done(((bf16[8,32,16,1024]{3,2,0,1:T(8,128)(2,1)}), bf16[8,32,16,1024]{3,2,0,1:T(8,128)(2,1)}, u32[]{:S(2)}, u32[]{:S(2)}) %all-to-all-start) | async-done | bytes 8388640 | tf_op jit(solution)/shard_map/all_to_all | solution.py:73
  208.1 8.5 %copy.30 = bf16[8,2,16,16,1024]{4,3,2,1,0:T(8,128)(2,1)} copy(bf16[8,2,16,16,1024]{4,3,0,1,2:T(8,128)(2,1)} %bitcast.15) | data formatting | bytes 16777216 | tf_op jit(solution)/shard_map/all_to_all | solution.py:73
  229.6 13.8 %fusion.1 = bf16[8,2,256,1024]{2,3,1,0:T(8,128)(2,1)} fusion(f32[8,2,256,512]{2,3,1,0:T(8,128)} %get-tuple-element.14, f32[8,2,256,512]{2,3,1,0:T(8,128)} %get-tuple-element.13, bf16[8,2,256,1024]{3,2,1,0:T(8,128)(2,1)} %bitcast.81), kind=kOutput, calls=%fused_computation.3 | convolution fusion | flops 2161115136 | bytes 33554432 | tf_op jit(solution)/shard_map/ky,czyx->czkx/dot_general | solution.py:41
  250.1 6.9 %slice_negate_fusion.1 = (f32[8,2,256,512]{2,3,1,0:T(8,128)}, f32[8,2,256,512]{2,3,1,0:T(8,128)}) fusion(f32[8,2,256,1024]{2,3,1,0:T(8,128)S(1)} %convolution_bitcast_fusion.2), kind=kLoop, calls=%fused_computation.14 | loop fusion | flops 2097152 | bytes 33554432 | tf_op jit(solution)/shard_map/neg | solution.py:43
  256.9 13.7 %fusion.2 = bf16[8,2,256,1024]{2,3,1,0:T(8,128)(2,1)} fusion(f32[8,2,256,512]{2,3,1,0:T(8,128)} %get-tuple-element.12, f32[8,2,256,512]{2,3,1,0:T(8,128)} %get-tuple-element.11, bf16[8,2,256,1024]{2,3,1,0:T(8,128)(2,1)} %fusion.1, pred[2,256,1024]{1,2,0:T(8,128)(4,1)S(1)} %pad_add_fusion), kind=kOutput, calls=%fused_computation.5 | convolution fusion | flops 2165309440 | bytes 34078720 | tf_op jit(solution)/shard_map/ky,czyx->czkx/dot_general | solution.py:41
  270.6 21.2 %copy.33 = bf16[8,2,256,1024]{3,1,0,2:T(2,128)(2,1)} copy(bf16[8,2,256,1024]{2,3,1,0:T(8,128)(2,1)} %fusion.2) | data formatting | bytes 16777216 | tf_op jit(solution)/shard_map/convert_element_type | solution.py:44
  304.6 87.2 %all-to-all-done.1 = bf16[8,2,256,1024]{3,1,0,2:T(2,128)(2,1)} async-done(((bf16[8,2,256,1024]{3,1,0,2:T(2,128)(2,1)}), bf16[8,2,256,1024]{3,1,0,2:T(2,128)(2,1)}, u32[]{:S(2)}, u32[]{:S(2)}) %all-to-all-start.1) | async-done | bytes 8388640 | tf_op jit(solution)/shard_map/all_to_all | solution.py:80
  391.9 11.3 %copy.34 = bf16[8,2,256,1024]{3,2,1,0:T(8,128)(2,1)} copy(bf16[8,2,256,1024]{3,1,0,2:T(2,128)(2,1)} %all-to-all-done.1) | data formatting | bytes 16777216 | tf_op jit(solution)/shard_map/all_to_all | solution.py:80
  403.2 16.3 %copy.35 = bf16[8,16,2,16,1024]{4,2,1,3,0:T(2,128)(2,1)} copy(bf16[8,16,2,16,1024]{4,3,1,2,0:T(8,128)(2,1)} %bitcast.82) | data formatting | bytes 16777216 | tf_op jit(solution)/shard_map/all_to_all | solution.py:80
  419.5 13.2 %all_to_all.33 = bf16[8,32,16,1024]{3,1,2,0:T(8,128)(2,1)} reshape(bf16[8,16,2,16,1024]{4,2,1,3,0:T(2,128)(2,1)} %copy.35) | data formatting | bytes 16777216 | tf_op jit(solution)/shard_map/all_to_all | solution.py:80
  438.5 6.8 %slice_negate_fusion = (f32[8,32,16,512]{3,1,2,0:T(8,128)}, f32[8,32,16,512]{3,1,2,0:T(8,128)}) fusion(f32[8,32,16,1024]{3,1,2,0:T(8,128)S(1)} %convolution_bitcast_fusion), kind=kLoop, calls=%fused_computation.13 | loop fusion | flops 2097152 | bytes 33554432 | tf_op jit(solution)/shard_map/neg | solution.py:43
  445.3 12.0 %fusion.3 = bf16[8,32,16,1024]{3,1,2,0:T(8,128)(2,1)} fusion(f32[8,32,16,512]{3,1,2,0:T(8,128)} %get-tuple-element.10, f32[8,32,16,512]{3,1,2,0:T(8,128)} %get-tuple-element.9, bf16[8,32,16,1024]{3,1,2,0:T(8,128)(2,1)} %all_to_all.33), kind=kOutput, calls=%fused_computation.7 | convolution fusion | flops 281034752 | bytes 33554432 | tf_op jit(solution)/shard_map/kz,czyx->ckyx/dot_general | solution.py:41
  457.3 17.3 %convert_convert_fusion = f32[8,32,16,1024]{3,2,1,0:T(8,128)} fusion(bf16[8,32,16,1024]{3,1,2,0:T(8,128)(2,1)} %fusion.3, bf16[512,512]{1,0:T(8,128)(2,1)S(1)} %get-tuple-element.20, bf16[512,512]{1,0:T(8,128)(2,1)S(1)} %fusion.43, bf16[512,512]{1,0:T(8,128)(2,1)S(1)} %multiply_convert_fusion), kind=kOutput, calls=%fused_computation.25 | convolution fusion | flops 8606711808 | bytes 26738688 | tf_op jit(solution)/shard_map/dot_general | solution.py:82
  474.6 18.5 %multiply_subtract_fusion = (f32[8,32,16,512]{3,2,1,0:T(8,128)}, f32[8,32,16,512]{3,2,1,0:T(8,128)}) fusion(f32[8,32,16,1024]{3,2,1,0:T(8,128)} %convert_convert_fusion, f32[8,32,16,1024]{3,2,1,0:T(8,128)} %convert_element_type.132), kind=kLoop, calls=%fused_computation.24 | loop fusion | flops 14680064 | bytes 50331648 | tf_op jit(solution)/shard_map/sub | solution.py:34
  493.1 8.3 %maximum_reduce_fusion = bf16[32,16,1024]{2,1,0:T(8,128)(2,1)} fusion(f32[8,32,16,512]{3,2,1,0:T(8,128)} %get-tuple-element.6, f32[8,32,16,512]{3,2,1,0:T(8,128)} %get-tuple-element.5), kind=kLoop, calls=%fused_computation.8 | loop fusion | flops 7864320 | bytes 17825792 | tf_op jit(solution)/shard_map/reduce_sum | solution.py:85
  501.4 106.7 %all-gather.3.cloned.1.call-done = bf16[256,16,1024]{2,1,0:T(8,128)(2,1)} async-done(((bf16[32,16,1024]{2,1,0:T(8,128)(2,1)}), bf16[256,16,1024]{2,1,0:T(8,128)(2,1)}) %all-gather.3.cloned.1.call-update) | async-done | bytes 8388624 | tf_op jit(solution)/shard_map/all_gather | solution.py:86
  (20 shorter events, 54.4 us)
Async XLA Ops:
  14.9 11.5 %copy-start = (bf16[32,16,1024]{2,1,0:T(8,128)(2,1)S(1)}, bf16[32,16,1024]{2,1,0:T(8,128)(2,1)}, u32[]{:S(2)}) copy-start(bf16[32,16,1024]{2,1,0:T(8,128)(2,1)} %param.3) | copy-start | bytes 3145732
  105.8 102.2 %all-to-all-start = ((bf16[8,32,16,1024]{3,2,0,1:T(8,128)(2,1)}), bf16[8,32,16,1024]{3,2,0,1:T(8,128)(2,1)}, u32[]{:S(2)}, u32[]{:S(2)}) async-start(bf16[8,32,16,1024]{3,2,0,1:T(8,128)(2,1)} %copy.28), calls=%async_computation | async-start | bytes 16777216 | tf_op jit(solution)/shard_map/all_to_all | solution.py:73
  291.8 100.1 %all-to-all-start.1 = ((bf16[8,2,256,1024]{3,1,0,2:T(2,128)(2,1)}), bf16[8,2,256,1024]{3,1,0,2:T(2,128)(2,1)}, u32[]{:S(2)}, u32[]{:S(2)}) async-start(bf16[8,2,256,1024]{3,1,0,2:T(2,128)(2,1)} %copy.33), calls=%async_computation.1 | async-start | bytes 16777216 | tf_op jit(solution)/shard_map/all_to_all | solution.py:80
  296.6 311.5 %all-gather.3.cloned.1.call-start = ((), (), s32[]{:S(2)}) async-start(), calls=%async_computation.2 | async-start | bytes 9437184 | tf_op jit(solution)/shard_map/all_gather | solution.py:86
Sparse Core Ops, SparseCore 0:
  501.5 106.5 all-gather.2
